TPU v7x, 256 devices: a whole 4x4x8 slice. The times are simulated.
256 devices in a mesh: row: 16 (over x, y), ka: 16 (over z, core).
Axes of the slice: x: 4, y: 4, z: 8, core: 2. Of those that a mesh axis runs over, the one named last changes fastest.
Arguments:
- t2: bfloat16 [16, 4096, 128], P('row', 'ka'), may hold values from -6 to 6
- vtiles: bfloat16 [16, 16, 160, 128, 128], P('row', 'ka'), may hold values from -0.078125 to 0.078125
- need_cd: int32 [16, 16, 64], P(None, 'ka'), may hold values from 0 to 255, as said below
- tile_cd: int32 [16, 16, 160], P('row', 'ka'), may hold values from 0 to 63
- tile_ab: int32 [16, 16, 160], P('row', 'ka'), may hold values from 0 to 63
Outputs:
- ladder: bfloat16 [1024, 16, 128], P(('row', 'ka'))
Inputs may be any that keep to these rules, and one draw needn't show every extreme that they name: `need_cd`: the 64 entries of one block's list are all different.
All inputs are finite; a program needn't handle non-finite values.
Results may differ from a plain program's by a relative error of at most 0.0015.
Values may be sent and summed in bfloat16 or wider, within the bound.
No kernel may reach another device: no remote copies, remote signals or barrier semaphores. Data moves between devices by JAX's collectives and lax.ppermute only.
A program may use at most 64 MiB of HBM per device.

v0:
```python
import jax
import jax.numpy as jnp
from jax import lax
from jax.sharding import PartitionSpec as P

AB_DEV = 64


def on_device(t2, vtiles, need_cd, tile_cd, tile_ab):
    pairs_all = t2.shape[0] * lax.axis_size("row")
    tile_edge = t2.shape[2]
    slot_cd = tile_cd[0, 0]
    slot_ab = tile_ab[0, 0]
    blocks = vtiles[0, 0]
    slot_count = slot_cd.shape[0]
    own_list = lax.dynamic_index_in_dim(need_cd[:, 0, :], lax.axis_index("row"), 0, keepdims=False)
    whole = lax.all_gather(t2, "row", axis=0, tiled=True)
    picked = jnp.take(whole, own_list[slot_cd], axis=1)
    products = jnp.einsum("pst,stu->spu", picked, blocks, preferred_element_type=jnp.float32)
    products = products.reshape(slot_count, pairs_all * tile_edge)
    upper_part = lax.optimization_barrier(products.astype(jnp.bfloat16))
    lower_part = (products - upper_part.astype(jnp.float32)).astype(jnp.bfloat16)
    share = AB_DEV // lax.axis_size("ka")
    wanted_rows = lax.iota(jnp.int32, share * lax.axis_size("ka"))
    onehot = (slot_ab[None, :] == wanted_rows[:, None]).astype(jnp.bfloat16)
    summed = jnp.dot(onehot, upper_part, preferred_element_type=jnp.float32)
    summed = summed + jnp.dot(onehot, lower_part, preferred_element_type=jnp.float32)
    reduced = lax.psum_scatter(
        summed.reshape(share * lax.axis_size("ka"), pairs_all, tile_edge),
        "ka",
        scatter_dimension=0,
        tiled=True,
    )
    return reduced.astype(jnp.bfloat16)


def solution(mesh):
    return jax.shard_map(
        on_device,
        mesh=mesh,
        in_specs=(
            P("row", "ka", None),
            P("row", "ka", None, None, None),
            P(None, "ka", None),
            P("row", "ka", None),
            P("row", "ka", None),
        ),
        out_specs=P(("row", "ka"), None, None),
        check_vma=False,
    )
```

profile of v0, /device:TPU:6, one launch (start us, length us, event | category | flops | bytes accessed | tf_op | source)
XLA Modules:
  0.0 133.9 jit_solution(1743452980378425177)
XLA Ops:
  6.5 0.0 copy-start
  6.5 0.0 all-gather.2.cloned.1.call-start
  6.5 0.7 all-gather.2.cloned.1.call-update
  7.3 0.0 reduce-scatter.2.cloned.1.call-start
  7.3 0.0 copy-done
  7.3 0.7 compare_select_fusion.1
  8.0 1.5 %gather_fusion = s32[160]{0:T(256)S(1)} fusion(s32[64]{0:T(128)S(1)} %dynamic-slice_bitcast_fusion, s32[1024]{0:T(1024)S(1)} %pad_clamp_fusion.1), kind=kCustom, calls=%fused_computation | custom fusion | bytes 1920 | tf_op jit(solution)/shard_map/gather | solution.py:18
  9.6 50.2 %all-gather.2.cloned.1.call-done = bf16[16,256,128]{2,1,0:T(8,128)(2,1)} async-done(((bf16[1,256,128]{2,1,0:T(8,128)(2,1)}), bf16[16,256,128]{2,1,0:T(8,128)(2,1)}) %all-gather.2.cloned.1.call-update) | async-done | bytes 1048592 | tf_op jit(solution)/shard_map/all_gather | solution.py:17
  59.8 1.9 %copy.8 = bf16[16,256,128]{2,0,1:T(8,128)(2,1)S(1)} copy(bf16[16,256,128]{2,1,0:T(8,128)(2,1)} %all-gather.2.cloned.1.call-done) | data formatting | bytes 2097152 | tf_op jit(solution)/shard_map/all_gather | solution.py:17
  61.7 0.7 gather_fusion.1
  62.5 3.5 %fusion = f32[160,16,128]{2,1,0:T(8,128)S(1)} fusion(bf16[1,1,160,128,128]{4,3,2,1,0:T(8,128)(2,1)} %param.6, bf16[160,16,128]{2,1,0:T(8,128)(2,1)S(1)} %gather_fusion.1, pred[160]{0:T(512)(128)(4,1)S(1)} %compare_and_fusion), kind=kOutput, calls=%fused_computation.2 | convolution fusion | flops 84213760 | bytes 7209120 | tf_op jit(solution)/shard_map/pst,stu->spu/dot_general | solution.py:19
  66.0 0.0 copy-start.1
  66.0 0.5 copy.14
  66.5 0.2 copy-done.1
  66.7 0.2 fusion.9
  66.9 0.6 fusion.3
  67.5 0.9 copy.10
  68.3 0.0 reduce-scatter.2.cloned.1.call-update
  68.4 57.3 %reduce-scatter.2.cloned.1.call-done = f32[4,16,128]{2,1,0:T(8,128)} async-done(((f32[64,16,128]{2,1,0:T(8,128)}), f32[4,16,128]{2,1,0:T(8,128)}) %reduce-scatter.2.cloned.1.call-update) | async-done | bytes 32784 | tf_op jit(solution)/shard_map/reduce_scatter | solution.py:28
  125.6 1.4 %convert_element_type.16 = bf16[4,16,128]{2,1,0:T(8,128)(2,1)} convert(f32[4,16,128]{2,1,0:T(8,128)} %reduce-scatter.2.cloned.1.call-done) | non-fusion elementwise | flops 8192 | bytes 49152 | tf_op jit(solution)/shard_map/convert_element_type | solution.py:34
  (5 shorter events, 0.0 us)
Async XLA Ops:
  6.5 0.8 copy-start
  6.5 53.3 %all-gather.2.cloned.1.call-start = ((), (), s32[]{:S(2)}) async-start(), calls=%async_computation.1 | async-start | bytes 1114112 | tf_op jit(solution)/shard_map/all_gather | solution.py:17
  7.3 118.4 %reduce-scatter.2.cloned.1.call-start = ((), (), s32[]{:S(2)}) async-start(), calls=%async_computation.2 | async-start | bytes 557056 | tf_op jit(solution)/shard_map/reduce_scatter | solution.py:28
  66.0 0.7 copy-start.1
Sparse Core Ops, SparseCore 0:
  9.8 50.0 all-gather.1
  68.5 57.1 reduce-scatter.1
where the time goes:
time: 134 us
  waiting for transfers between devices  108 us (81%)
  between operations  13.5 us (10%)
  local copies, waits for them, and re-layouts  5.76 us (4%)
  matrix products  4.26 us (3%)
  other arithmetic  2.08 us (2%)
    reduce_scatter x1, waiting for transfers between devices, on_device(): lax.psum_scatter(summed.reshape(share * lax.axis_size('ka'), pairs_all, t...  57.3 us
    all_gather x1, waiting for transfers between devices, on_device(): whole = lax.all_gather(t2, 'row', axis=0, tiled=True)  50.2 us
    dot_general x1, matrix products, on_device(): jnp.einsum('pst,stu->spu', picked, blocks, preferred_element_type=jnp.flo...  3.47 us
  transfers between devices with their start and end apart: 2, of which 2 were waited for; matrix products, arithmetic and copies ran while one was open for 2% of the time, Pallas kernels for 0%

commit v1 on v0

--- a/solution.py
+++ b/solution.py
@@ -14,7 +14,9 @@
     blocks = vtiles[0, 0]
     slot_count = slot_cd.shape[0]
     own_list = lax.dynamic_index_in_dim(need_cd[:, 0, :], lax.axis_index("row"), 0, keepdims=False)
-    whole = lax.all_gather(t2, "row", axis=0, tiled=True)
+    whole = jnp.concatenate(
+        lax.all_to_all(jnp.stack([t2] * lax.axis_size("row")), "row", 0, 0), axis=0
+    )
     picked = jnp.take(whole, own_list[slot_cd], axis=1)
     products = jnp.einsum("pst,stu->spu", picked, blocks, preferred_element_type=jnp.float32)
     products = products.reshape(slot_count, pairs_all * tile_edge)

time: 134 us -> 106 us (0.79)
  waiting for transfers between devices: 108 us -> 72.3 us
  starting transfers between devices: 0.04 us -> 7.59 us
    all_gather x1 -> x0, waiting for transfers between devices: 50.2 us -> none  [on_device(): whole = lax.all_gather(t2, 'row', axis=0, tiled=True)]
    all_to_all x0 -> x1, waiting for transfers between devices: none -> 13.5 us  [on_device(): lax.all_to_all(jnp.stack([t2] * lax.axis_size('row')), 'row', 0, 0)]
    all_to_all x0 -> x1, starting transfers between devices: none -> 7.56 us  [on_device(): lax.all_to_all(jnp.stack([t2] * lax.axis_size('row')), 'row', 0, 0)]
    another operation x0 -> x1, local copies, waits for them, and re-layouts: none -> 2.03 us  [on_device(): jnp.stack([t2] * lax.axis_size('row'))]
    all_gather x1 -> x0, local copies, waits for them, and re-layouts: 1.9 us -> none  [on_device(): whole = lax.all_gather(t2, 'row', axis=0, tiled=True)]
    reduce_scatter x1, waiting for transfers between devices: 57.3 us -> 58.8 us  [on_device(): lax.psum_scatter(summed.reshape(share * lax.axis_size('ka'), pairs_all, t...]
where the time goes in v1:
time: 106 us
  waiting for transfers between devices  72.3 us (68%)
  between operations  13.5 us (13%)
  starting transfers between devices  7.59 us (7%)
  local copies, waits for them, and re-layouts  6.57 us (6%)
  matrix products  4.27 us (4%)
  other arithmetic  1.39 us (1%)
    reduce_scatter x1, waiting for transfers between devices, on_device(): lax.psum_scatter(summed.reshape(share * lax.axis_size('ka'), pairs_all, t...  58.8 us
    all_to_all x1, waiting for transfers between devices, on_device(): lax.all_to_all(jnp.stack([t2] * lax.axis_size('row')), 'row', 0, 0)  13.5 us
    all_to_all x1, starting transfers between devices, on_device(): lax.all_to_all(jnp.stack([t2] * lax.axis_size('row')), 'row', 0, 0)  7.56 us
    dot_general x1, matrix products, on_device(): jnp.einsum('pst,stu->spu', picked, blocks, preferred_element_type=jnp.flo...  3.47 us
    gather x2, local copies, waits for them, and re-layouts, on_device(): picked = jnp.take(whole, own_list[slot_cd], axis=1)  2.3 us
  transfers between devices with their start and end apart: 2, of which 2 were waited for; matrix products, arithmetic and copies ran while one was open for 2% of the time, Pallas kernels for 0%

profile of v1, /device:TPU:6, one launch (start us, length us, event | category | flops | bytes accessed | tf_op | source)
XLA Modules:
  0.0 105.7 jit_solution(17192712103504274295)
XLA Ops:
  6.5 0.0 copy-start
  6.5 2.0 %stack.2 = bf16[16,1,256,128]{3,2,1,0:T(8,128)(2,1)} broadcast(bf16[256,128]{1,0:T(8,128)(2,1)} %bitcast.36), dimensions={2,3} | broadcast | bytes 1114112 | tf_op jit(solution)/shard_map/stack | solution.py:18
  8.6 0.0 copy-start.2
  8.6 7.6 %all-to-all-start = ((bf16[16,1,256,128]{3,2,1,0:T(8,128)(2,1)}), bf16[16,1,256,128]{3,2,1,0:T(8,128)(2,1)S(1)}, u32[]{:S(2)}, u32[]{:S(2)}) async-start(bf16[16,1,256,128]{3,2,1,0:T(8,128)(2,1)} %stack.2), calls=%async_computation | async-start | bytes 2097152 | tf_op jit(solution)/shard_map/all_to_all | solution.py:18
  16.1 0.0 reduce-scatter.2.cloned.1.call-start
  16.2 0.0 copy-done
  16.2 0.0 copy-done.2
  16.2 1.6 %gather_fusion = s32[160]{0:T(256)S(1)} fusion(s32[64]{0:T(128)S(1)} %dynamic-slice_bitcast_fusion, s32[1024]{0:T(1024)S(1)} %pad_clamp_fusion.1), kind=kCustom, calls=%fused_computation | custom fusion | bytes 1920 | tf_op jit(solution)/shard_map/gather | solution.py:20
  17.8 13.5 %all-to-all-done = bf16[16,1,256,128]{3,2,1,0:T(8,128)(2,1)S(1)} async-done(((bf16[16,1,256,128]{3,2,1,0:T(8,128)(2,1)}), bf16[16,1,256,128]{3,2,1,0:T(8,128)(2,1)S(1)}, u32[]{:S(2)}, u32[]{:S(2)}) %all-to-all-start) | async-done | bytes 1048608 | tf_op jit(solution)/shard_map/all_to_all | solution.py:18
  31.4 0.7 copy.14
  32.0 0.7 gather_fusion.1
  32.8 3.5 %fusion = f32[160,16,128]{2,1,0:T(8,128)S(1)} fusion(bf16[1,1,160,128,128]{4,3,2,1,0:T(8,128)(2,1)} %param.6, bf16[160,16,128]{2,1,0:T(8,128)(2,1)S(1)} %gather_fusion.1, pred[160]{0:T(512)(128)(4,1)S(1)} %compare_and_fusion), kind=kOutput, calls=%fused_computation.2 | convolution fusion | flops 84213760 | bytes 7209120 | tf_op jit(solution)/shard_map/pst,stu->spu/dot_general | solution.py:21
  36.3 0.0 copy-start.1
  36.3 0.5 copy.13
  36.8 0.2 copy-done.1
  36.9 0.2 fusion.9
  37.2 0.6 fusion.3
  37.8 0.9 copy.8
  38.6 0.0 reduce-scatter.2.cloned.1.call-update
  38.7 58.8 %reduce-scatter.2.cloned.1.call-done = f32[4,16,128]{2,1,0:T(8,128)} async-done(((f32[64,16,128]{2,1,0:T(8,128)}), f32[4,16,128]{2,1,0:T(8,128)}) %reduce-scatter.2.cloned.1.call-update) | async-done | bytes 32784 | tf_op jit(solution)/shard_map/reduce_scatter | solution.py:30
  97.5 1.4 %convert_element_type.16 = bf16[4,16,128]{2,1,0:T(8,128)(2,1)} convert(f32[4,16,128]{2,1,0:T(8,128)} %reduce-scatter.2.cloned.1.call-done) | non-fusion elementwise | flops 8192 | bytes 49152 | tf_op jit(solution)/shard_map/convert_element_type | solution.py:36
  (6 shorter events, 0.0 us)
Async XLA Ops:
  6.5 9.6 %copy-start = (s32[16,1,64]{2,1,0:T(1,128)S(1)}, s32[16,1,64]{2,1,0:T(1,128)}, u32[]{:S(2)}) copy-start(s32[16,1,64]{2,1,0:T(1,128)} %param.7) | copy-start | bytes 12292
  8.6 7.6 %copy-start.2 = (s32[1,1,160]{2,1,0:T(1,128)S(1)}, s32[1,1,160]{2,1,0:T(1,128)}, u32[]{:S(2)}) copy-start(s32[1,1,160]{2,1,0:T(1,128)} %param.8) | copy-start | bytes 1924
  8.6 22.8 %all-to-all-start = ((bf16[16,1,256,128]{3,2,1,0:T(8,128)(2,1)}), bf16[16,1,256,128]{3,2,1,0:T(8,128)(2,1)S(1)}, u32[]{:S(2)}, u32[]{:S(2)}) async-start(bf16[16,1,256,128]{3,2,1,0:T(8,128)(2,1)} %stack.2), calls=%async_computation | async-start | bytes 2097152 | tf_op jit(solution)/shard_map/all_to_all | solution.py:18
  16.1 81.3 %reduce-scatter.2.cloned.1.call-start = ((), (), s32[]{:S(2)}) async-start(), calls=%async_computation.2 | async-start | bytes 557056 | tf_op jit(solution)/shard_map/reduce_scatter | solution.py:30
  36.3 0.7 copy-start.1
Sparse Core Ops, SparseCore 0:
  38.8 58.6 reduce-scatter.1
